TPU v7x, 128 devices: a whole 4x4x4 slice. The times are simulated.
128 devices in a mesh: lat: 4 (over z), lon: 32 (over x, y, core).
Axes of the slice: x: 4, y: 4, z: 4, core: 2. Of those that a mesh axis runs over, the one named last changes fastest.
Arguments:
- column_state: float32 [4, 32, 128, 4096], P(None, None, 'lat', 'lon'), may hold values from -6 to 6
- wind_speed: float32 [2, 32, 128, 4096], P(None, None, 'lat', 'lon'), may hold values from -0.4 to 0.4
- diffusivity: float32 [32, 128, 4096], P(None, 'lat', 'lon'), may hold values from 0.02 to 0.2
- batch_index: int32 [4, 131072, 1], P('lat', 'lon'), may hold values from 0 to 31; in each aligned block of 4096 rows (0 to 4095, 4096 to 8191, ..., all dimensions but the last counted through in order) at most 256 rows name the same one
- input_weight: bfloat16 [32, 512, 128], P('lon'), may hold values from -0.5 to 0.5
- middle_weight: bfloat16 [32, 3, 512, 512], P('lon'), may hold values from -0.25 to 0.25
- output_weight: bfloat16 [32, 128, 512], P('lon'), may hold values from -0.25 to 0.25
Outputs:
- new_state: float32 [4, 32, 128, 4096], P(None, None, 'lat', 'lon')
Inputs may be any that keep to these rules, and one draw needn't show every extreme that they name: `batch_index`: within the columns of one device no batch is named more than 256 times; some device names some batch exactly 256 times.
All inputs are finite; a program needn't handle non-finite values.
Results may differ from a plain program's by a relative error of at most 0.0012.
Values may be sent and summed in bfloat16 or wider, within the bound.
No kernel may reach another device: no remote copies, remote signals or barrier semaphores. Data moves between devices by JAX's collectives and lax.ppermute only.
A program may use at most 128 MiB of HBM per device.

v0:
```python
import jax
import jax.numpy as jnp
from jax import lax
from jax.sharding import PartitionSpec as P


def shifted(axis, pieces, periodic):
    count = lax.axis_size(axis)
    forward = [(i, i + 1) for i in range(count - 1)]
    if periodic:
        forward.append((count - 1, 0))
    backward = [(target, source) for source, target in forward]
    low_parts, high_parts = pieces
    low = lax.ppermute(low_parts, axis, forward)
    high = lax.ppermute(high_parts, axis, backward)
    return (low, high)


def pack(arrays):
    flat = jnp.concatenate([a.reshape(-1) for a in arrays])
    return flat


def unpack(flat, shapes):
    out, start = ([], 0)
    for shape in shapes:
        size = 1
        for s in shape:
            size *= s
        out.append(flat[start : start + size].reshape(shape))
        start += size
    return out


def advect(extended, east_wind, north_wind, spread):
    middle = extended[:, :, 1:-1, 1:-1]
    north_cell = extended[:, :, 2:, 1:-1]
    south_cell = extended[:, :, :-2, 1:-1]
    east_cell = extended[:, :, 1:-1, 2:]
    west_cell = extended[:, :, 1:-1, :-2]
    return (
        middle
        - 0.5 * east_wind * (east_cell - west_cell)
        - 0.5 * north_wind * (north_cell - south_cell)
        + spread * (east_cell + west_cell + north_cell + south_cell - 4.0 * middle)
    )


def widen(q, fields):
    v, l, rows, cols = q.shape
    top = [q[:, :, rows - 2 :, :]] + [f[:, rows - 1 :, :] for f in fields]
    bottom = [q[:, :, :2, :]] + [f[:, :1, :] for f in fields]
    lat_shapes = [a.shape for a in top]
    low, high = shifted("lat", (pack(top), pack(bottom)), False)
    low, high = (unpack(low, lat_shapes), unpack(high, lat_shapes))
    q = jnp.concatenate([low[0], q, high[0]], axis=2)
    fields = [jnp.concatenate([lo, f, hi], axis=1) for lo, f, hi in zip(low[1:], fields, high[1:])]
    east = [jnp.swapaxes(q[..., cols - 2 :], -1, -2)] + [
        jnp.swapaxes(f[..., cols - 1 :], -1, -2) for f in fields
    ]
    west = [jnp.swapaxes(q[..., :2], -1, -2)] + [jnp.swapaxes(f[..., :1], -1, -2) for f in fields]
    lon_shapes = [a.shape for a in east]
    low, high = shifted("lon", (pack(east), pack(west)), True)
    low, high = (unpack(low, lon_shapes), unpack(high, lon_shapes))
    q = jnp.concatenate([jnp.swapaxes(low[0], -1, -2), q, jnp.swapaxes(high[0], -1, -2)], axis=3)
    fields = [
        jnp.concatenate([jnp.swapaxes(lo, -1, -2), f, jnp.swapaxes(hi, -1, -2)], axis=2)
        for lo, f, hi in zip(low[1:], fields, high[1:])
    ]
    return (q, fields)


def positions(targets_all, experts):
    count = targets_all.shape[0]
    block = 128
    onehot = (targets_all[:, None] == jnp.arange(experts, dtype=jnp.int32)[None, :]).astype(
        jnp.bfloat16
    )
    blocks = onehot.reshape(count // block, block, experts)
    rows = jnp.arange(block, dtype=jnp.int32)
    before = (rows[:, None] > rows[None, :]).astype(jnp.bfloat16)
    within = jnp.einsum("ij,bje->bie", before, blocks, preferred_element_type=jnp.float32)
    totals = jnp.sum(blocks.astype(jnp.float32), axis=1)
    offsets = jnp.cumsum(totals, axis=0) - totals
    ranks = within + offsets[:, None, :]
    position = jnp.sum(ranks * blocks.astype(jnp.float32), axis=2)
    return position.reshape(count).astype(jnp.int32)


def local(
    column_state, wind_speed, diffusivity, batch_index, input_weight, middle_weight, output_weight
):
    num_vars, levels, lat_cells, lon_cells = column_state.shape
    q, (east_wind, north_wind, spread) = widen(
        column_state, [wind_speed[0], wind_speed[1], diffusivity]
    )
    first = advect(q, east_wind, north_wind, spread)
    lat_index = lax.axis_index("lat")
    lat_count = lax.axis_size("lat")
    row = jnp.arange(lat_cells + 2)[None, None, :, None]
    outside = (row == 0) & (lat_index == 0) | (row == lat_cells + 1) & (lat_index == lat_count - 1)
    first = jnp.where(outside, 0.0, first)
    current = advect(
        first, east_wind[:, 1:-1, 1:-1], north_wind[:, 1:-1, 1:-1], spread[:, 1:-1, 1:-1]
    )
    features = num_vars * levels
    column_count = lat_cells * lon_cells
    columns = current.reshape(features, column_count).astype(jnp.bfloat16)
    experts = lax.axis_size("lon")
    capacity = 2 * column_count // experts
    targets_all = batch_index.reshape(column_count)
    position = positions(targets_all, experts)
    targets = targets_all * capacity + position
    packed = jnp.zeros((features, experts * capacity), jnp.bfloat16).at[:, targets].set(columns)
    packed = packed.reshape(features, experts, capacity)
    received = lax.all_to_all(packed, "lon", split_axis=1, concat_axis=1, tiled=True)
    layout = received.shape
    flattened = received.reshape(layout[0], layout[1] * layout[2])
    hidden = jax.nn.silu(
        jnp.dot(input_weight[0], flattened, preferred_element_type=jnp.float32)
    ).astype(jnp.bfloat16)
    for layer_index in range(middle_weight.shape[1]):
        hidden = jax.nn.silu(
            jnp.dot(middle_weight[0, layer_index], hidden, preferred_element_type=jnp.float32)
        ).astype(jnp.bfloat16)
    result = jnp.dot(output_weight[0], hidden, preferred_element_type=jnp.float32).astype(
        jnp.bfloat16
    )
    answered = result.reshape(layout)
    returned = lax.all_to_all(answered, "lon", split_axis=1, concat_axis=1, tiled=True)
    tendency = returned.reshape(features, -1)[:, targets]
    return current + tendency.astype(jnp.float32).reshape(current.shape)


def solution(mesh):
    in_specs = (
        P(None, None, "lat", "lon"),
        P(None, None, "lat", "lon"),
        P(None, "lat", "lon"),
        P("lat", "lon", None),
        P("lon", None, None),
        P("lon", None, None, None),
        P("lon", None, None),
    )
    out_specs = P(None, None, "lat", "lon")
    return jax.shard_map(local, mesh=mesh, in_specs=in_specs, out_specs=out_specs, check_vma=False)
```

profile of v0, /device:TPU:96, one launch (start us, length us, event | category | flops | bytes accessed | tf_op | source)
XLA Modules:
  0.0 221.6 jit_solution(11655371338631515701)
XLA Ops:
  0.0 1.0 fusion.58
  1.1 1.3 fusion.55
  2.4 2.5 %multiply_bitcast_fusion.1 = (f32[32,32,128]{2,1,0:T(8,128)}, f32[32,32,128]{2,1,0:T(8,128)}, f32[32,32,128]{2,1,0:T(8,128)S(1)}, f32[32,32,128]{2,1,0:T(8,128)S(1)}) fusion(f32[2,32,32,128]{3,2,1,0:T(8,128)} %param.8), kind=kLoop, calls=%fused_computation.75 | loop fusion | flops 262144 | bytes 3145728 | tf_op jit(solution)/shard_map/mul | solution.py:43
  4.9 2.3 %collective-permute-start.1 = (f32[45056]{0:T(1024)S(1)}, f32[45056]{0:T(1024)S(1)}, u32[]{:S(2)}, u32[]{:S(2)}) collective-permute-start(f32[45056]{0:T(1024)S(1)} %pad_maximum_fusion.13), channel_id=1, source_target_pairs={{32,0},{64,32},{96,64},{33,1},{65,33},{97,65},{34,2},{66,34},{98,6... | collective-permute-start | bytes 540680 | tf_op jit(solution)/shard_map/ppermute | solution.py:15
  7.3 1.3 collective-permute-start
  8.6 0.2 convert_reduce_fusion
  8.8 0.3 fusion.31
  9.1 0.6 compare_select_fusion
  9.8 1.2 collective-permute-done.1
  11.0 4.1 %collective-permute-done = f32[45056]{0:T(1024)S(1)} collective-permute-done((f32[45056]{0:T(1024)S(1)}, f32[45056]{0:T(1024)S(1)}, u32[]{:S(2)}, u32[]{:S(2)}) %collective-permute-start) | collective-permute-done | bytes 180256 | tf_op jit(solution)/shard_map/ppermute | solution.py:14
  15.3 0.6 slice_reduce_fusion.4
  15.9 0.7 reshape_transpose.19
  16.6 0.7 reshape_transpose.22
  17.3 1.3 pad_maximum_fusion.11
  18.6 0.6 slice_reduce_fusion.3
  19.2 0.7 reshape_transpose.20
  19.9 0.7 reshape_transpose.23
  20.7 0.6 slice_reduce_fusion.5
  21.3 0.7 reshape_transpose.18
  22.0 0.7 reshape_transpose.21
  22.7 0.9 slice.263
  23.6 0.9 slice.260
  24.6 0.4 pad_maximum_fusion.7
  24.9 2.3 %slice_bitcast_fusion.1 = (f32[4,32,2,36]{2,3,1,0:T(8,128)}, f32[4,32,2,36]{2,3,1,0:T(8,128)S(1)}) fusion(f32[4,32,36,128]{3,2,1,0:T(8,128)S(1)} %pad_maximum_fusion.7), kind=kLoop, calls=%fused_computation.40 | loop fusion | bytes 147456 | tf_op jit(solution)/shard_map/transpose | solution.py:58
  27.3 3.4 %copy.10 = f32[4,32,2,36]{3,2,1,0:T(2,128)} copy(f32[4,32,2,36]{2,3,1,0:T(8,128)} %get-tuple-element.13) | data formatting | bytes 73728 | tf_op jit(solution)/shard_map/transpose | solution.py:58
  30.7 1.7 reshape.253
  32.4 1.4 concatenate.64
  33.8 1.7 copy.11
  35.5 1.1 reshape.255
  36.6 0.8 concatenate.65
  37.4 5.1 %collective-permute-start.3 = (f32[12480]{0:T(1024)S(1)}, f32[12480]{0:T(1024)S(1)}, u32[]{:S(2)}, u32[]{:S(2)}) collective-permute-start(f32[12480]{0:T(1024)S(1)} %concatenate.65), channel_id=1, source_target_pairs={{1,0},{2,1},{3,2},{4,3},{5,4},{6,5},{7,6},{8,7},{9,8},{10,9},{11,1... | collective-permute-start | bytes 149768 | tf_op jit(solution)/shard_map/ppermute | solution.py:15
  42.5 0.5 and_or_fusion
  43.0 0.8 slice.274
  43.8 0.9 reshape.254
  44.7 0.9 reshape.256
  45.6 1.1 concatenate.77
  46.7 0.9 fusion.61
  47.6 1.1 concatenate.76
  48.7 1.1 transpose_reshape.13
  49.8 1.1 concatenate.79
  50.9 1.1 transpose_reshape.12
  52.0 1.1 concatenate.78
  53.1 1.9 copy.13
  55.0 3.4 %copy.12 = f32[4,32,36,2]{3,2,1,0:T(8,128)} copy(f32[4,32,36,2]{2,3,1,0:T(2,128)} %bitcast.162) | data formatting | bytes 73728 | tf_op jit(solution)/shard_map/transpose | solution.py:65
  58.5 3.4 %pad_maximum_fusion.8 = f32[32,34,130]{2,1,0:T(8,128)} fusion(f32[32,34,1]{2,1,0:T(8,128)} %transpose_reshape.13, f32[32,1,128]{2,1,0:T(1,128)} %bitcast.173, f32[32,32,128]{2,1,0:T(8,128)} %param.9, f32[32,1,128]{2,1,0:T(1,128)} %bitcast.175, f32[32,34,1]{2,1,0:T(8,128)} %transpose_reshape.12), kind=kLoop, calls=%fused_computation.47 | loop fusion | flops 565760 | bytes 1131520 | tf_op jit(solution)/shard_map/concatenate | solution.py:67
  61.9 5.2 %pad_maximum_fusion.6 = f32[4,32,36,132]{3,2,1,0:T(8,128)S(1)} fusion(f32[4,32,36,2]{3,2,1,0:T(8,128)S(1)} %copy.13, f32[4,32,2,128]{3,2,1,0:T(2,128)S(1)} %bitcast.153, f32[4,32,32,128]{3,2,1,0:T(8,128)} %param.7, f32[4,32,2,128]{3,2,1,0:T(2,128)S(1)} %bitcast.156, f32[4,32,36,2]{3,2,1,0:T(8,128)S(1)} %copy-done.2), kind=kLoop, calls=%fused_computation.36 | loop fusion | flops 2433024 | bytes 4866048 | tf_op jit(solution)/shard_map/concatenate | solution.py:65
  67.3 2.9 %maximum_multiply_fusion = (f32[32,34,130]{2,1,0:T(8,128)}, f32[32,34,130]{2,1,0:T(8,128)}) fusion(f32[32,34,1]{2,1,0:T(8,128)S(1)} %copy-done.9, f32[32,1,128]{2,1,0:T(1,128)S(1)} %bitcast.167, f32[32,32,128]{2,1,0:T(8,128)S(1)} %copy-done.7, f32[32,1,128]{2,1,0:T(1,128)S(1)} %bitcast.171, f32[32,34,1]{2,1,0:T(8,128)S(1)} %copy-done.10, ...), kind=kLoop, calls=%fused_computation.45 | loop fusion | flops 1414400 | bytes 2263040 | tf_op jit(solution)/shard_map/mul | solution.py:43
  70.2 8.9 %add_select_fusion = f32[4,32,34,130]{3,2,1,0:T(8,128)S(1)} fusion(f32[4,32,36,132]{3,2,1,0:T(8,128)S(1)} %pad_maximum_fusion.6, f32[4,32,36,2]{3,2,1,0:T(8,128)S(1)} %copy.13, f32[4,32,2,128]{3,2,1,0:T(2,128)S(1)} %bitcast.154, f32[4,32,32,128]{3,2,1,0:T(8,128)S(1)} %copy-done.4, f32[4,32,2,128]{3,2,1,0:T(2,128)S(1)} %bitcast.157, ...), kind=kLoop, calls=%fused_computation.37 | loop fusion | flops 11315200 | bytes 13182498 | tf_op jit(solution)/shard_map/jit(_where)/select_n | solution.py:102
  79.1 4.3 %fusion.54 = (bf16[4,32,32,128]{3,2,1,0:T(8,128)(2,1)S(1)}, f32[4,32,32,128]{3,2,1,0:T(8,128)}) fusion(f32[32,32,128]{2,1,0:T(8,128)S(1)} %copy-done.8, f32[4,32,34,130]{3,2,1,0:T(8,128)S(1)} %add_select_fusion, f32[32,32,128]{2,1,0:T(8,128)} %get-tuple-element.18, f32[32,32,128]{2,1,0:T(8,128)S(1)} %copy-done.13), kind=kLoop, calls=%fused_computation.92 | loop fusion | flops 7340032 | bytes 15204352 | tf_op jit(solution)/shard_map/convert_element_type | solution.py:108
  83.4 0.5 copy.27
  83.9 0.7 copy.22
  84.6 11.5 %scatter_custom_fusion = bf16[128,8192]{0,1:T(8,128)(2,1)S(1)} fusion(s32[4096]{0:T(1024)S(1)} %bitcast.178, bf16[128,4096]{0,1:T(8,128)(2,1)S(1)} %copy.22, bf16[]{:T(256)} %constant.11.clone.1), kind=kCustom, calls=%fused_computation.53 | custom fusion | bytes 3145730 | tf_op jit(solution)/shard_map/scatter | solution.py:114
  96.1 34.3 %all_to_all.10 = bf16[128,32,256]{0,2,1:T(8,128)(2,1)} all-to-all(bf16[128,32,256]{0,2,1:T(8,128)(2,1)S(1)} %bitcast.148), channel_id=1, replica_groups=mesh['lat'=4,'lon'=32] {'lon'}, dimensions={1} | all-to-all | bytes 4194304 | tf_op jit(solution)/shard_map/all_to_all | solution.py:116
  130.4 13.5 %fusion.20 = f32[8192,512]{1,0:T(8,128)} fusion(bf16[128,8192]{0,1:T(8,128)(2,1)} %bitcast.159, bf16[1,3,512,512]{3,2,1,0:T(8,128)(2,1)} %param.12, bf16[1,512,128]{2,1,0:T(8,128)(2,1)S(1)} %copy-done), kind=kOutput, calls=%fused_computation.29 | convolution fusion | flops 5389680640 | bytes 19529728 | tf_op jit(solution)/shard_map/dot_general | solution.py:124
  143.9 11.6 %fusion.18 = f32[8192,512]{1,0:T(8,128)} fusion(f32[8192,512]{1,0:T(8,128)} %fusion.20, bf16[1,3,512,512]{3,2,1,0:T(8,128)(2,1)S(1)} %copy-done.27), kind=kOutput, calls=%fused_computation.28 | convolution fusion | flops 4315938816 | bytes 34078720 | tf_op jit(solution)/shard_map/dot_general | solution.py:124
  155.5 15.0 %convolution_convert_fusion = bf16[8192,128]{1,0:T(8,128)(2,1)} fusion(f32[8192,512]{1,0:T(8,128)} %fusion.18, bf16[1,3,512,512]{3,2,1,0:T(8,128)(2,1)S(1)} %copy-done.27, bf16[1,128,512]{2,1,0:T(8,128)(2,1)S(1)} %copy-done.28), kind=kOutput, calls=%fused_computation.26 | convolution fusion | flops 5411700736 | bytes 19529728 | tf_op jit(solution)/shard_map/dot_general | solution.py:126
  170.5 4.0 %all-to-all-start.1 = ((bf16[128,32,256]{0,2,1:T(8,128)(2,1)}), bf16[128,32,256]{0,2,1:T(8,128)(2,1)S(1)}, u32[]{:S(2)}, u32[]{:S(2)}) async-start(bf16[128,32,256]{0,2,1:T(8,128)(2,1)} %bitcast.158), calls=%async_computation.1 | async-start | bytes 4194304 | tf_op jit(solution)/shard_map/all_to_all | solution.py:130
  174.6 28.9 %all-to-all-done.1 = bf16[128,32,256]{0,2,1:T(8,128)(2,1)S(1)} async-done(((bf16[128,32,256]{0,2,1:T(8,128)(2,1)}), bf16[128,32,256]{0,2,1:T(8,128)(2,1)S(1)}, u32[]{:S(2)}, u32[]{:S(2)}) %all-to-all-start.1) | async-done | bytes 2097184 | tf_op jit(solution)/shard_map/all_to_all | solution.py:130
  203.5 12.1 %gather_fusion = bf16[4096,128]{1,0:T(8,128)(2,1)S(1)} fusion(bf16[128,8192]{0,1:T(8,128)(2,1)S(1)} %bitcast.146, s32[4096]{0:T(1024)S(1)} %broadcast_clamp_fusion), kind=kCustom, calls=%fused_computation | custom fusion | bytes 2113536 | tf_op jit(solution)/shard_map/gather | solution.py:131
  215.6 0.1 convert_bitcast_fusion
  215.8 1.8 copy.23
  217.6 2.1 copy.25
  219.7 0.1 copy-done.5
  219.8 1.8 bitcast_add_fusion
  (74 shorter events, 0.5 us)
Async XLA Ops:
  0.0 130.4 %copy-start = (bf16[1,512,128]{2,1,0:T(8,128)(2,1)S(1)}, bf16[1,512,128]{2,1,0:T(8,128)(2,1)}, u32[]{:S(2)}) copy-start(bf16[1,512,128]{2,1,0:T(8,128)(2,1)} %param.11) | copy-start | bytes 393220
  0.0 8.6 %copy-start.24 = (s32[1,4096,1]{1,2,0:T(1,128)S(1)}, s32[1,4096,1]{1,2,0:T(1,128)}, u32[]{:S(2)}) copy-start(s32[1,4096,1]{1,2,0:T(1,128)} %param.10) | copy-start | bytes 49156
  4.8 15.8 %copy-start.6 = (f32[32,32,128]{2,1,0:T(8,128)}, f32[32,32,128]{2,1,0:T(8,128)S(1)}, u32[]{:S(2)}) copy-start(f32[32,32,128]{2,1,0:T(8,128)S(1)} %get-tuple-element.20) | copy-start | bytes 1572868
  4.9 6.1 %collective-permute-start.1 = (f32[45056]{0:T(1024)S(1)}, f32[45056]{0:T(1024)S(1)}, u32[]{:S(2)}, u32[]{:S(2)}) collective-permute-start(f32[45056]{0:T(1024)S(1)} %pad_maximum_fusion.13), channel_id=1, source_target_pairs={{32,0},{64,32},{96,64},{33,1},{65,33},{97,65},{34,2},{66,34},{98,6... | collective-permute-start | bytes 540680 | tf_op jit(solution)/shard_map/ppermute | solution.py:15
  7.3 7.9 %collective-permute-start = (f32[45056]{0:T(1024)S(1)}, f32[45056]{0:T(1024)S(1)}, u32[]{:S(2)}, u32[]{:S(2)}) collective-permute-start(f32[45056]{0:T(1024)S(1)} %pad_maximum_fusion.12), channel_id=1, source_target_pairs={{0,32},{32,64},{64,96},{1,33},{33,65},{65,97},{2,34},{34,66},{66,9... | collective-permute-start | bytes 540680 | tf_op jit(solution)/shard_map/ppermute | solution.py:14
  11.0 6.3 %copy-start.14 = (f32[45056]{0:T(1024)}, f32[45056]{0:T(1024)S(1)}, u32[]{:S(2)}) copy-start(f32[45056]{0:T(1024)S(1)} %collective-permute-done.1) | copy-start | bytes 540676
  11.0 8.2 %copy-start.22 = (f32[4096]{0:T(1024)}, f32[4096]{0:T(1024)S(1)}, u32[]{:S(2)}) copy-start(f32[4096]{0:T(1024)S(1)} %get-tuple-element.30) | copy-start | bytes 49156
  11.0 9.6 %copy-start.16 = (f32[4096]{0:T(1024)}, f32[4096]{0:T(1024)S(1)}, u32[]{:S(2)}) copy-start(f32[4096]{0:T(1024)S(1)} %get-tuple-element.32) | copy-start | bytes 49156
  15.2 2.1 copy-start.15
  15.2 5.5 %copy-start.18 = (f32[4096]{0:T(1024)}, f32[4096]{0:T(1024)S(1)}, u32[]{:S(2)}) copy-start(f32[4096]{0:T(1024)S(1)} %get-tuple-element.28) | copy-start | bytes 49156
  15.2 5.5 %copy-start.20 = (f32[4096]{0:T(1024)}, f32[4096]{0:T(1024)S(1)}, u32[]{:S(2)}) copy-start(f32[4096]{0:T(1024)S(1)} %get-tuple-element.29) | copy-start | bytes 49156
  15.2 5.5 %copy-start.23 = (f32[4096]{0:T(1024)}, f32[4096]{0:T(1024)S(1)}, u32[]{:S(2)}) copy-start(f32[4096]{0:T(1024)S(1)} %get-tuple-element.27) | copy-start | bytes 49156
  17.3 7.3 %copy-start.3 = (f32[4,32,32,128]{3,2,1,0:T(8,128)S(1)}, f32[4,32,32,128]{3,2,1,0:T(8,128)}, u32[]{:S(2)}) copy-start(f32[4,32,32,128]{3,2,1,0:T(8,128)} %param.7) | copy-start | bytes 6291460
  33.8 9.2 %collective-permute-start.2 = (f32[12480]{0:T(1024)}, f32[12480]{0:T(1024)}, u32[]{:S(2)}, u32[]{:S(2)}) collective-permute-start(f32[12480]{0:T(1024)} %concatenate.64), channel_id=1, source_target_pairs={{0,1},{1,2},{2,3},{3,4},{4,5},{5,6},{6,7},{7,8},{8,9},{9,10},{10,1... | collective-permute-start | bytes 149768 | tf_op jit(solution)/shard_map/ppermute | solution.py:14
  37.4 7.2 %collective-permute-start.3 = (f32[12480]{0:T(1024)S(1)}, f32[12480]{0:T(1024)S(1)}, u32[]{:S(2)}, u32[]{:S(2)}) collective-permute-start(f32[12480]{0:T(1024)S(1)} %concatenate.65), channel_id=1, source_target_pairs={{1,0},{2,1},{3,2},{4,3},{5,4},{6,5},{7,6},{8,7},{9,8},{10,9},{11,1... | collective-permute-start | bytes 149768 | tf_op jit(solution)/shard_map/ppermute | solution.py:15
  58.5 3.4 %copy-start.2 = (f32[4,32,36,2]{3,2,1,0:T(8,128)S(1)}, f32[4,32,36,2]{3,2,1,0:T(8,128)}, u32[]{:S(2)}) copy-start(f32[4,32,36,2]{3,2,1,0:T(8,128)} %copy.12) | copy-start | bytes 110596
  61.9 5.3 %copy-start.7 = (f32[32,32,128]{2,1,0:T(8,128)S(1)}, f32[32,32,128]{2,1,0:T(8,128)}, u32[]{:S(2)}) copy-start(f32[32,32,128]{2,1,0:T(8,128)} %copy-done.6) | copy-start | bytes 1572868
  61.9 5.3 %copy-start.9 = (f32[32,34,1]{2,1,0:T(8,128)S(1)}, f32[32,34,1]{2,1,0:T(8,128)}, u32[]{:S(2)}) copy-start(f32[32,34,1]{2,1,0:T(8,128)} %concatenate.77) | copy-start | bytes 13060
  61.9 5.3 %copy-start.10 = (f32[32,34,1]{2,1,0:T(8,128)S(1)}, f32[32,34,1]{2,1,0:T(8,128)}, u32[]{:S(2)}) copy-start(f32[32,34,1]{2,1,0:T(8,128)} %concatenate.76) | copy-start | bytes 13060
  61.9 5.3 %copy-start.11 = (f32[32,34,1]{2,1,0:T(8,128)S(1)}, f32[32,34,1]{2,1,0:T(8,128)}, u32[]{:S(2)}) copy-start(f32[32,34,1]{2,1,0:T(8,128)} %concatenate.79) | copy-start | bytes 13060
  61.9 5.3 %copy-start.12 = (f32[32,34,1]{2,1,0:T(8,128)S(1)}, f32[32,34,1]{2,1,0:T(8,128)}, u32[]{:S(2)}) copy-start(f32[32,34,1]{2,1,0:T(8,128)} %concatenate.78) | copy-start | bytes 13060
  61.9 5.3 %copy-start.17 = (f32[4096]{0:T(1024)S(1)}, f32[4096]{0:T(1024)}, u32[]{:S(2)}) copy-start(f32[4096]{0:T(1024)} %copy-done.16) | copy-start | bytes 49156
  61.9 5.3 %copy-start.19 = (f32[4096]{0:T(1024)S(1)}, f32[4096]{0:T(1024)}, u32[]{:S(2)}) copy-start(f32[4096]{0:T(1024)} %copy-done.18) | copy-start | bytes 49156
  61.9 5.3 %copy-start.21 = (f32[4096]{0:T(1024)S(1)}, f32[4096]{0:T(1024)}, u32[]{:S(2)}) copy-start(f32[4096]{0:T(1024)} %copy-done.20) | copy-start | bytes 49156
  67.3 2.9 %copy-start.4 = (f32[4,32,32,128]{3,2,1,0:T(8,128)S(1)}, f32[4,32,32,128]{3,2,1,0:T(8,128)}, u32[]{:S(2)}) copy-start(f32[4,32,32,128]{3,2,1,0:T(8,128)} %param.7) | copy-start | bytes 6291460
  67.3 2.9 %copy-start.26 = (pred[34]{0:T(512)(128)(4,1)S(1)}, pred[34]{0:T(512)(128)(4,1)}, u32[]{:S(2)}) copy-start(pred[34]{0:T(512)(128)(4,1)} %and_or_fusion) | copy-start | bytes 106
  70.2 8.9 %copy-start.8 = (f32[32,32,128]{2,1,0:T(8,128)S(1)}, f32[32,32,128]{2,1,0:T(8,128)}, u32[]{:S(2)}) copy-start(f32[32,32,128]{2,1,0:T(8,128)} %param.9) | copy-start | bytes 1572868
  70.2 8.9 %copy-start.13 = (f32[32,32,128]{2,1,0:T(8,128)S(1)}, f32[32,32,128]{2,1,0:T(8,128)}, u32[]{:S(2)}) copy-start(f32[32,32,128]{2,1,0:T(8,128)} %get-tuple-element.17) | copy-start | bytes 1572868
  83.4 1.1 copy-start.25
  130.4 13.5 %copy-start.27 = (bf16[1,3,512,512]{3,2,1,0:T(8,128)(2,1)S(1)}, bf16[1,3,512,512]{3,2,1,0:T(8,128)(2,1)}, u32[]{:S(2)}) copy-start(bf16[1,3,512,512]{3,2,1,0:T(8,128)(2,1)} %param.12) | copy-start | bytes 4718596
  143.9 11.6 %copy-start.28 = (bf16[1,128,512]{2,1,0:T(8,128)(2,1)S(1)}, bf16[1,128,512]{2,1,0:T(8,128)(2,1)}, u32[]{:S(2)}) copy-start(bf16[1,128,512]{2,1,0:T(8,128)(2,1)} %param.13) | copy-start | bytes 393220
  170.5 33.0 %all-to-all-start.1 = ((bf16[128,32,256]{0,2,1:T(8,128)(2,1)}), bf16[128,32,256]{0,2,1:T(8,128)(2,1)S(1)}, u32[]{:S(2)}, u32[]{:S(2)}) async-start(bf16[128,32,256]{0,2,1:T(8,128)(2,1)} %bitcast.158), calls=%async_computation.1 | async-start | bytes 4194304 | tf_op jit(solution)/shard_map/all_to_all | solution.py:130
  217.6 2.2 %copy-start.5 = (f32[4,32,32,128]{3,2,1,0:T(8,128)S(1)}, f32[4,32,32,128]{3,2,1,0:T(8,128)}, u32[]{:S(2)}) copy-start(f32[4,32,32,128]{3,2,1,0:T(8,128)} %get-tuple-element.12) | copy-start | bytes 6291460
  219.7 1.9 copy-start.1
where the time goes:
time: 222 us
  local copies, waits for them, and re-layouts  67 us (30%)
  matrix products  40.4 us (18%)
  waiting for transfers between devices  34.3 us (15%)
  blocking collectives  34.3 us (15%)
  other arithmetic  32.5 us (15%)
  starting transfers between devices  12.7 us (6%)
    all_to_all x1, blocking collectives, local(): lax.all_to_all(packed, 'lon', split_axis=1, concat_axis=1, tiled=True)  34.3 us
    all_to_all x1, waiting for transfers between devices, local(): lax.all_to_all(answered, 'lon', split_axis=1, concat_axis=1, tiled=True)  28.9 us
    dot_general x2, matrix products, local(): jnp.dot(middle_weight[0, layer_index], hidden, preferred_element_type=jnp...  25.1 us
    dot_general x1, matrix products, local(): jnp.dot(output_weight[0], hidden, preferred_element_type=jnp.float32)  15 us
    gather x1, local copies, waits for them, and re-layouts, local(): tendency = returned.reshape(features, -1)[:, targets]  12.1 us
    scatter x1, local copies, waits for them, and re-layouts, local(): jnp.zeros((features, experts * capacity), jnp.bfloat16).at[:, targets]  11.5 us
    select_n x1, other arithmetic, local(): first = jnp.where(outside, 0.0, first)  8.9 us
    ppermute x2, starting transfers between devices, shifted(): high = lax.ppermute(high_parts, axis, backward)  7.38 us
  transfers between devices with their start and end apart: 5, of which 3 were waited for; matrix products, arithmetic and copies ran while one was open for 3% of the time, Pallas kernels for 0%

commit v1 on v0

--- a/solution.py
+++ b/solution.py
@@ -127,7 +127,10 @@
         jnp.bfloat16
     )
     answered = result.reshape(layout)
-    returned = lax.all_to_all(answered, "lon", split_axis=1, concat_axis=1, tiled=True)
+    returned = jnp.concatenate(
+        lax.all_to_all(jnp.stack(jnp.split(answered, lax.axis_size("lon"), axis=1)), "lon", 0, 0),
+        axis=1,
+    )
     tendency = returned.reshape(features, -1)[:, targets]
     return current + tendency.astype(jnp.float32).reshape(current.shape)
 

time: 222 us -> 241 us (1.086)
  local copies, waits for them, and re-layouts: 67 us -> 87 us
    unnamed x60 -> x91, local copies, waits for them, and re-layouts: 2.77 us -> 22.1 us
where the time goes in v1:
time: 241 us; the launch traced here: 240 us
  local copies, waits for them, and re-layouts  87 us (36%)
  matrix products  39.5 us (16%)
  waiting for transfers between devices  34.3 us (14%)
  blocking collectives  34.3 us (14%)
  other arithmetic  31.3 us (13%)
  starting transfers between devices  12.9 us (5%)
    all_to_all x1, blocking collectives, local(): lax.all_to_all(packed, 'lon', split_axis=1, concat_axis=1, tiled=True)  34.3 us
    all_to_all x1, waiting for transfers between devices, local(): lax.all_to_all(jnp.stack(jnp.split(answered, lax.axis_size('lon'), axis=1...  28.9 us
    dot_general x2, matrix products, local(): jnp.dot(middle_weight[0, layer_index], hidden, preferred_element_type=jnp...  25 us
    unnamed x91, local copies, waits for them, and re-layouts  22.1 us
    dot_general x1, matrix products, local(): jnp.dot(output_weight[0], hidden, preferred_element_type=jnp.float32)  14.3 us
    gather x1, local copies, waits for them, and re-layouts, local(): tendency = returned.reshape(features, -1)[:, targets]  12.1 us
    scatter x1, local copies, waits for them, and re-layouts, local(): jnp.zeros((features, experts * capacity), jnp.bfloat16).at[:, targets]  11.5 us
    select_n x1, other arithmetic, local(): first = jnp.where(outside, 0.0, first)  8.9 us
  transfers between devices with their start and end apart: 5, of which 3 were waited for; matrix products, arithmetic and copies ran while one was open for 3% of the time, Pallas kernels for 0%

profile of v1, /device:TPU:96, one launch (start us, length us, event | category | flops | bytes accessed | tf_op | source)
XLA Modules:
  0.0 239.8 jit_solution(11516809730464948124)
XLA Ops:
  0.0 1.0 fusion.90
  1.0 1.3 fusion.87
  2.4 2.5 %multiply_bitcast_fusion.1 = (f32[32,32,128]{2,1,0:T(8,128)}, f32[32,32,128]{2,1,0:T(8,128)}, f32[32,32,128]{2,1,0:T(8,128)S(1)}, f32[32,32,128]{2,1,0:T(8,128)S(1)}) fusion(f32[2,32,32,128]{3,2,1,0:T(8,128)} %param.8), kind=kLoop, calls=%fused_computation.75 | loop fusion | flops 262144 | bytes 3145728 | tf_op jit(solution)/shard_map/mul | solution.py:43
  4.9 2.4 %collective-permute-start.1 = (f32[45056]{0:T(1024)S(1)}, f32[45056]{0:T(1024)S(1)}, u32[]{:S(2)}, u32[]{:S(2)}) collective-permute-start(f32[45056]{0:T(1024)S(1)} %pad_maximum_fusion.13), channel_id=1, source_target_pairs={{32,0},{64,32},{96,64},{33,1},{65,33},{97,65},{34,2},{66,34},{98,6... | collective-permute-start | bytes 540680 | tf_op jit(solution)/shard_map/ppermute | solution.py:15
  7.4 1.3 collective-permute-start
  9.3 0.6 compare_select_fusion
  9.9 1.2 collective-permute-done.1
  11.2 4.1 %collective-permute-done = f32[45056]{0:T(1024)S(1)} collective-permute-done((f32[45056]{0:T(1024)S(1)}, f32[45056]{0:T(1024)S(1)}, u32[]{:S(2)}, u32[]{:S(2)}) %collective-permute-start) | collective-permute-done | bytes 180256 | tf_op jit(solution)/shard_map/ppermute | solution.py:14
  16.0 0.7 reshape_transpose.19
  16.7 0.7 reshape_transpose.22
  18.2 0.7 reshape_transpose.20
  18.9 0.7 reshape_transpose.23
  20.3 0.7 reshape_transpose.18
  21.0 0.7 reshape_transpose.21
  21.7 0.9 slice.263
  22.6 0.9 slice.260
  23.9 2.3 slice_bitcast_fusion.1
  26.3 3.4 %copy.10 = f32[4,32,2,36]{3,2,1,0:T(2,128)} copy(f32[4,32,2,36]{2,3,1,0:T(8,128)} %get-tuple-element.13) | data formatting | bytes 73728 | tf_op jit(solution)/shard_map/transpose | solution.py:58
  29.6 1.7 reshape.253
  31.3 1.4 concatenate.64
  32.8 1.7 copy.11
  34.4 1.1 reshape.255
  35.6 0.8 concatenate.65
  36.4 5.1 %collective-permute-start.3 = (f32[12480]{0:T(1024)S(1)}, f32[12480]{0:T(1024)S(1)}, u32[]{:S(2)}, u32[]{:S(2)}) collective-permute-start(f32[12480]{0:T(1024)S(1)} %concatenate.65), channel_id=1, source_target_pairs={{1,0},{2,1},{3,2},{4,3},{5,4},{6,5},{7,6},{8,7},{9,8},{10,9},{11,1... | collective-permute-start | bytes 149768 | tf_op jit(solution)/shard_map/ppermute | solution.py:15
  42.0 0.8 slice.274
  42.7 0.9 reshape.254
  43.6 0.9 reshape.256
  44.6 1.1 concatenate.77
  45.7 0.9 fusion.93
  46.5 1.1 concatenate.76
  47.7 1.1 transpose_reshape.13
  48.8 1.1 concatenate.79
  49.9 1.1 transpose_reshape.12
  51.0 1.1 concatenate.78
  52.1 1.9 copy.13
  54.0 3.4 %copy.12 = f32[4,32,36,2]{3,2,1,0:T(8,128)} copy(f32[4,32,36,2]{2,3,1,0:T(2,128)} %bitcast.323) | data formatting | bytes 73728 | tf_op jit(solution)/shard_map/transpose | solution.py:65
  57.4 3.4 %pad_maximum_fusion.8 = f32[32,34,130]{2,1,0:T(8,128)} fusion(f32[32,34,1]{2,1,0:T(8,128)} %transpose_reshape.13, f32[32,1,128]{2,1,0:T(1,128)} %bitcast.334, f32[32,32,128]{2,1,0:T(8,128)} %param.9, f32[32,1,128]{2,1,0:T(1,128)} %bitcast.336, f32[32,34,1]{2,1,0:T(8,128)} %transpose_reshape.12), kind=kLoop, calls=%fused_computation.47 | loop fusion | flops 565760 | bytes 1131520 | tf_op jit(solution)/shard_map/concatenate | solution.py:67
  60.9 5.2 %pad_maximum_fusion.6 = f32[4,32,36,132]{3,2,1,0:T(8,128)S(1)} fusion(f32[4,32,36,2]{3,2,1,0:T(8,128)S(1)} %copy.13, f32[4,32,2,128]{3,2,1,0:T(2,128)S(1)} %bitcast.283, f32[4,32,32,128]{3,2,1,0:T(8,128)} %param.7, f32[4,32,2,128]{3,2,1,0:T(2,128)S(1)} %bitcast.286, f32[4,32,36,2]{3,2,1,0:T(8,128)S(1)} %copy-done.2), kind=kLoop, calls=%fused_computation.36 | loop fusion | flops 2433024 | bytes 4866048 | tf_op jit(solution)/shard_map/concatenate | solution.py:65
  66.2 2.9 %maximum_multiply_fusion = (f32[32,34,130]{2,1,0:T(8,128)}, f32[32,34,130]{2,1,0:T(8,128)}) fusion(f32[32,34,1]{2,1,0:T(8,128)S(1)} %copy-done.10, f32[32,1,128]{2,1,0:T(1,128)S(1)} %bitcast.328, f32[32,32,128]{2,1,0:T(8,128)S(1)} %copy-done.7, f32[32,1,128]{2,1,0:T(1,128)S(1)} %bitcast.332, f32[32,34,1]{2,1,0:T(8,128)S(1)} %copy-done.11, ...), kind=kLoop, calls=%fused_computation.45 | loop fusion | flops 1414400 | bytes 2263040 | tf_op jit(solution)/shard_map/mul | solution.py:43
  69.2 8.9 %add_select_fusion = f32[4,32,34,130]{3,2,1,0:T(8,128)S(1)} fusion(f32[4,32,36,132]{3,2,1,0:T(8,128)S(1)} %pad_maximum_fusion.6, f32[4,32,36,2]{3,2,1,0:T(8,128)S(1)} %copy.13, f32[4,32,2,128]{3,2,1,0:T(2,128)S(1)} %bitcast.284, f32[4,32,32,128]{3,2,1,0:T(8,128)S(1)} %copy-done.4, f32[4,32,2,128]{3,2,1,0:T(2,128)S(1)} %bitcast.287, ...), kind=kLoop, calls=%fused_computation.37 | loop fusion | flops 11315200 | bytes 13182498 | tf_op jit(solution)/shard_map/jit(_where)/select_n | solution.py:102
  78.1 4.3 %fusion.86 = (bf16[4,32,32,128]{3,2,1,0:T(8,128)(2,1)S(1)}, f32[4,32,32,128]{3,2,1,0:T(8,128)}) fusion(f32[32,32,128]{2,1,0:T(8,128)S(1)} %copy-done.9, f32[4,32,34,130]{3,2,1,0:T(8,128)S(1)} %add_select_fusion, f32[32,32,128]{2,1,0:T(8,128)} %get-tuple-element.18, f32[32,32,128]{2,1,0:T(8,128)S(1)} %copy-done.14), kind=kLoop, calls=%fused_computation.156 | loop fusion | flops 7340032 | bytes 15204352 | tf_op jit(solution)/shard_map/convert_element_type | solution.py:108
  82.9 0.7 copy.22
  83.5 11.5 %scatter_custom_fusion = bf16[128,8192]{0,1:T(8,128)(2,1)S(1)} fusion(s32[4096]{0:T(1024)S(1)} %bitcast.339, bf16[128,4096]{0,1:T(8,128)(2,1)S(1)} %copy.22, bf16[]{:T(256)} %constant.11.clone.1), kind=kCustom, calls=%fused_computation.53 | custom fusion | bytes 3145730 | tf_op jit(solution)/shard_map/scatter | solution.py:114
  95.0 34.3 %all_to_all.10 = bf16[128,32,256]{0,2,1:T(8,128)(2,1)} all-to-all(bf16[128,32,256]{0,2,1:T(8,128)(2,1)S(1)} %bitcast.278), channel_id=1, replica_groups=mesh['lat'=4,'lon'=32] {'lon'}, dimensions={1} | all-to-all | bytes 4194304 | tf_op jit(solution)/shard_map/all_to_all | solution.py:116
  129.4 13.4 %fusion.20 = f32[8192,512]{1,0:T(8,128)} fusion(bf16[128,8192]{0,1:T(8,128)(2,1)} %bitcast.320, bf16[1,3,512,512]{3,2,1,0:T(8,128)(2,1)} %param.12, bf16[1,512,128]{2,1,0:T(8,128)(2,1)S(1)} %copy-done), kind=kOutput, calls=%fused_computation.29 | convolution fusion | flops 5389680640 | bytes 19529728 | tf_op jit(solution)/shard_map/dot_general | solution.py:124
  142.8 11.6 %fusion.18 = f32[8192,512]{1,0:T(8,128)} fusion(f32[8192,512]{1,0:T(8,128)} %fusion.20, bf16[1,3,512,512]{3,2,1,0:T(8,128)(2,1)} %param.12), kind=kOutput, calls=%fused_computation.28 | convolution fusion | flops 4315938816 | bytes 34078720 | tf_op jit(solution)/shard_map/dot_general | solution.py:124
  154.4 14.3 %convolution_convert_fusion = bf16[8192,128]{1,0:T(8,128)(2,1)S(1)} fusion(f32[8192,512]{1,0:T(8,128)} %fusion.18, bf16[1,3,512,512]{3,2,1,0:T(8,128)(2,1)} %param.12, bf16[1,128,512]{2,1,0:T(8,128)(2,1)S(1)} %copy-done.28), kind=kOutput, calls=%fused_computation.26 | convolution fusion | flops 5411700736 | bytes 19529728 | tf_op jit(solution)/shard_map/dot_general | solution.py:126
  168.6 0.6 fusion.79
  171.8 0.6 fusion.74
  173.6 0.6 fusion.71
  174.3 0.6 fusion.70
  175.5 0.6 fusion.68
  176.1 0.6 fusion.67
  177.4 0.6 fusion.65
  185.5 0.6 fusion.52
  186.8 0.6 fusion.50
  187.4 0.6 fusion.49
  188.0 0.6 fusion.48
  188.6 4.1 %all-to-all-start.1 = ((bf16[32,128,1,256]{1,3,2,0:T(8,128)(2,1)}), bf16[32,128,1,256]{1,3,2,0:T(8,128)(2,1)S(1)}, u32[]{:S(2)}, u32[]{:S(2)}) async-start(bf16[32,128,1,256]{1,3,2,0:T(8,128)(2,1)} %fusion.48), calls=%async_computation.1 | async-start | bytes 4194304 | tf_op jit(solution)/shard_map/all_to_all | solution.py:131
  192.7 28.9 %all-to-all-done.1 = bf16[32,128,1,256]{1,3,2,0:T(8,128)(2,1)S(1)} async-done(((bf16[32,128,1,256]{1,3,2,0:T(8,128)(2,1)}), bf16[32,128,1,256]{1,3,2,0:T(8,128)(2,1)S(1)}, u32[]{:S(2)}, u32[]{:S(2)}) %all-to-all-start.1) | async-done | bytes 2097184 | tf_op jit(solution)/shard_map/all_to_all | solution.py:131
  221.6 12.1 %gather_fusion = bf16[4096,128]{1,0:T(8,128)(2,1)S(1)} fusion(bf16[128,8192]{0,1:T(8,128)(2,1)S(1)} %bitcast.276, s32[4096]{0:T(1024)S(1)} %broadcast_clamp_fusion), kind=kCustom, calls=%fused_computation | custom fusion | bytes 2113536 | tf_op jit(solution)/shard_map/gather | solution.py:134
  233.9 1.8 copy.23
  235.7 2.1 copy.25
  238.0 1.8 bitcast_add_fusion
  (106 shorter events, 17.6 us)
Async XLA Ops:
  0.0 129.4 %copy-start = (bf16[1,512,128]{2,1,0:T(8,128)(2,1)S(1)}, bf16[1,512,128]{2,1,0:T(8,128)(2,1)}, u32[]{:S(2)}) copy-start(bf16[1,512,128]{2,1,0:T(8,128)(2,1)} %param.11) | copy-start | bytes 393220
  2.3 6.4 %copy-start.25 = (s32[1,4096,1]{1,2,0:T(1,128)S(1)}, s32[1,4096,1]{1,2,0:T(1,128)}, u32[]{:S(2)}) copy-start(s32[1,4096,1]{1,2,0:T(1,128)} %param.10) | copy-start | bytes 49156
  4.8 14.8 %copy-start.6 = (f32[32,32,128]{2,1,0:T(8,128)}, f32[32,32,128]{2,1,0:T(8,128)S(1)}, u32[]{:S(2)}) copy-start(f32[32,32,128]{2,1,0:T(8,128)S(1)} %get-tuple-element.20) | copy-start | bytes 1572868
  4.9 12.5 %copy-start.8 = (f32[32,32,128]{2,1,0:T(8,128)S(1)}, f32[32,32,128]{2,1,0:T(8,128)}, u32[]{:S(2)}) copy-start(f32[32,32,128]{2,1,0:T(8,128)} %param.9) | copy-start | bytes 1572868
  4.9 6.2 %collective-permute-start.1 = (f32[45056]{0:T(1024)S(1)}, f32[45056]{0:T(1024)S(1)}, u32[]{:S(2)}, u32[]{:S(2)}) collective-permute-start(f32[45056]{0:T(1024)S(1)} %pad_maximum_fusion.13), channel_id=1, source_target_pairs={{32,0},{64,32},{96,64},{33,1},{65,33},{97,65},{34,2},{66,34},{98,6... | collective-permute-start | bytes 540680 | tf_op jit(solution)/shard_map/ppermute | solution.py:15
  7.4 7.9 %collective-permute-start = (f32[45056]{0:T(1024)S(1)}, f32[45056]{0:T(1024)S(1)}, u32[]{:S(2)}, u32[]{:S(2)}) collective-permute-start(f32[45056]{0:T(1024)S(1)} %pad_maximum_fusion.12), channel_id=1, source_target_pairs={{0,32},{32,64},{64,96},{1,33},{33,65},{65,97},{2,34},{34,66},{66,9... | collective-permute-start | bytes 540680 | tf_op jit(solution)/shard_map/ppermute | solution.py:14
  11.2 6.3 %copy-start.15 = (f32[45056]{0:T(1024)}, f32[45056]{0:T(1024)S(1)}, u32[]{:S(2)}) copy-start(f32[45056]{0:T(1024)S(1)} %collective-permute-done.1) | copy-start | bytes 540676
  11.2 6.3 %copy-start.23 = (f32[4096]{0:T(1024)}, f32[4096]{0:T(1024)S(1)}, u32[]{:S(2)}) copy-start(f32[4096]{0:T(1024)S(1)} %get-tuple-element.30) | copy-start | bytes 49156
  11.2 8.4 %copy-start.17 = (f32[4096]{0:T(1024)}, f32[4096]{0:T(1024)S(1)}, u32[]{:S(2)}) copy-start(f32[4096]{0:T(1024)S(1)} %get-tuple-element.32) | copy-start | bytes 49156
  15.3 2.1 copy-start.16
  15.3 2.1 copy-start.19
  15.3 2.1 copy-start.24
  15.3 4.3 %copy-start.21 = (f32[4096]{0:T(1024)}, f32[4096]{0:T(1024)S(1)}, u32[]{:S(2)}) copy-start(f32[4096]{0:T(1024)S(1)} %get-tuple-element.29) | copy-start | bytes 49156
  17.6 6.0 %copy-start.3 = (f32[4,32,32,128]{3,2,1,0:T(8,128)S(1)}, f32[4,32,32,128]{3,2,1,0:T(8,128)}, u32[]{:S(2)}) copy-start(f32[4,32,32,128]{3,2,1,0:T(8,128)} %param.7) | copy-start | bytes 6291460
  32.8 9.2 %collective-permute-start.2 = (f32[12480]{0:T(1024)}, f32[12480]{0:T(1024)}, u32[]{:S(2)}, u32[]{:S(2)}) collective-permute-start(f32[12480]{0:T(1024)} %concatenate.64), channel_id=1, source_target_pairs={{0,1},{1,2},{2,3},{3,4},{4,5},{5,6},{6,7},{7,8},{8,9},{9,10},{10,1... | collective-permute-start | bytes 149768 | tf_op jit(solution)/shard_map/ppermute | solution.py:14
  36.4 7.2 %collective-permute-start.3 = (f32[12480]{0:T(1024)S(1)}, f32[12480]{0:T(1024)S(1)}, u32[]{:S(2)}, u32[]{:S(2)}) collective-permute-start(f32[12480]{0:T(1024)S(1)} %concatenate.65), channel_id=1, source_target_pairs={{1,0},{2,1},{3,2},{4,3},{5,4},{6,5},{7,6},{8,7},{9,8},{10,9},{11,1... | collective-permute-start | bytes 149768 | tf_op jit(solution)/shard_map/ppermute | solution.py:15
  57.4 3.4 %copy-start.2 = (f32[4,32,36,2]{3,2,1,0:T(8,128)S(1)}, f32[4,32,36,2]{3,2,1,0:T(8,128)}, u32[]{:S(2)}) copy-start(f32[4,32,36,2]{3,2,1,0:T(8,128)} %copy.12) | copy-start | bytes 110596
  60.8 5.3 %copy-start.7 = (f32[32,32,128]{2,1,0:T(8,128)S(1)}, f32[32,32,128]{2,1,0:T(8,128)}, u32[]{:S(2)}) copy-start(f32[32,32,128]{2,1,0:T(8,128)} %copy-done.6) | copy-start | bytes 1572868
  60.8 5.3 %copy-start.10 = (f32[32,34,1]{2,1,0:T(8,128)S(1)}, f32[32,34,1]{2,1,0:T(8,128)}, u32[]{:S(2)}) copy-start(f32[32,34,1]{2,1,0:T(8,128)} %concatenate.77) | copy-start | bytes 13060
  60.8 5.3 %copy-start.11 = (f32[32,34,1]{2,1,0:T(8,128)S(1)}, f32[32,34,1]{2,1,0:T(8,128)}, u32[]{:S(2)}) copy-start(f32[32,34,1]{2,1,0:T(8,128)} %concatenate.76) | copy-start | bytes 13060
  60.8 5.3 %copy-start.12 = (f32[32,34,1]{2,1,0:T(8,128)S(1)}, f32[32,34,1]{2,1,0:T(8,128)}, u32[]{:S(2)}) copy-start(f32[32,34,1]{2,1,0:T(8,128)} %concatenate.79) | copy-start | bytes 13060
  60.8 5.3 %copy-start.13 = (f32[32,34,1]{2,1,0:T(8,128)S(1)}, f32[32,34,1]{2,1,0:T(8,128)}, u32[]{:S(2)}) copy-start(f32[32,34,1]{2,1,0:T(8,128)} %concatenate.78) | copy-start | bytes 13060
  60.9 5.3 %copy-start.18 = (f32[4096]{0:T(1024)S(1)}, f32[4096]{0:T(1024)}, u32[]{:S(2)}) copy-start(f32[4096]{0:T(1024)} %copy-done.17) | copy-start | bytes 49156
  60.9 5.3 %copy-start.20 = (f32[4096]{0:T(1024)S(1)}, f32[4096]{0:T(1024)}, u32[]{:S(2)}) copy-start(f32[4096]{0:T(1024)} %copy-done.19) | copy-start | bytes 49156
  60.9 5.3 %copy-start.22 = (f32[4096]{0:T(1024)S(1)}, f32[4096]{0:T(1024)}, u32[]{:S(2)}) copy-start(f32[4096]{0:T(1024)} %copy-done.21) | copy-start | bytes 49156
  66.2 2.9 %copy-start.4 = (f32[4,32,32,128]{3,2,1,0:T(8,128)S(1)}, f32[4,32,32,128]{3,2,1,0:T(8,128)}, u32[]{:S(2)}) copy-start(f32[4,32,32,128]{3,2,1,0:T(8,128)} %param.7) | copy-start | bytes 6291460
  66.2 2.9 %copy-start.27 = (pred[34]{0:T(512)(128)(4,1)S(1)}, pred[34]{0:T(512)(128)(4,1)}, u32[]{:S(2)}) copy-start(pred[34]{0:T(512)(128)(4,1)} %and_or_fusion) | copy-start | bytes 106
  69.2 8.9 %copy-start.9 = (f32[32,32,128]{2,1,0:T(8,128)S(1)}, f32[32,32,128]{2,1,0:T(8,128)}, u32[]{:S(2)}) copy-start(f32[32,32,128]{2,1,0:T(8,128)} %param.9) | copy-start | bytes 1572868
  69.2 8.9 %copy-start.14 = (f32[32,32,128]{2,1,0:T(8,128)S(1)}, f32[32,32,128]{2,1,0:T(8,128)}, u32[]{:S(2)}) copy-start(f32[32,32,128]{2,1,0:T(8,128)} %get-tuple-element.17) | copy-start | bytes 1572868
  82.4 1.1 copy-start.26
  142.8 11.6 %copy-start.28 = (bf16[1,128,512]{2,1,0:T(8,128)(2,1)S(1)}, bf16[1,128,512]{2,1,0:T(8,128)(2,1)}, u32[]{:S(2)}) copy-start(bf16[1,128,512]{2,1,0:T(8,128)(2,1)} %param.13) | copy-start | bytes 393220
  188.6 33.0 %all-to-all-start.1 = ((bf16[32,128,1,256]{1,3,2,0:T(8,128)(2,1)}), bf16[32,128,1,256]{1,3,2,0:T(8,128)(2,1)S(1)}, u32[]{:S(2)}, u32[]{:S(2)}) async-start(bf16[32,128,1,256]{1,3,2,0:T(8,128)(2,1)} %fusion.48), calls=%async_computation.1 | async-start | bytes 4194304 | tf_op jit(solution)/shard_map/all_to_all | solution.py:131
  235.7 2.2 copy-start.5
  237.9 1.9 copy-start.1
